TPU v7x, 256 devices: a whole 4x4x8 slice. The times are simulated.
256 devices in a mesh: row: 16 (over z, core), col: 16 (over x, y).
Axes of the slice: x: 4, y: 4, z: 8, core: 2. Of those that a mesh axis runs over, the one named last changes fastest.
Arguments:
- site_tensor: bfloat16 [1024, 4, 1024], P('row', None, 'col'), may hold values from -180 to 180
- site_tangent: bfloat16 [1024, 4, 1024], P('row', None, 'col'), may hold values from -180 to 180
- left_env: bfloat16 [1024, 16384], P('row', 'col'), may hold values from -0.1875 to 0.375
- right_env: bfloat16 [1024, 16384], P('row', 'col'), may hold values from -0.046875 to 0.09375
- mpo: bfloat16 [16, 16, 4, 4], replicated, may hold values from -0.25 to 0.75
- dissipation: float32 [4], replicated, may hold values from 0.2 to 2
Outputs:
- evolved: float32 [1024, 4, 1024], P('row', None, 'col')
- evolved_tangent: float32 [1024, 4, 1024], P('row', None, 'col')
All inputs are finite; a program needn't handle non-finite values.
Results may differ from a plain program's by a relative error of at most 0.0055.
Values may be sent and summed in bfloat16 or wider, within the bound.
No kernel may reach another device: no remote copies, remote signals or barrier semaphores. Data moves between devices by JAX's collectives and lax.ppermute only.
A program may use at most 64 MiB of HBM per device.

v0:
```python
import jax
import jax.numpy as jnp
from jax import lax
from jax.sharding import PartitionSpec as P

KRYLOV = 3
taylor_order = 16


def inner(first, second):
    return jnp.sum(first * second)


def taylor(hess, dhess):
    size = hess.shape[0]
    term = jnp.zeros((size,), jnp.float32).at[0].set(1.0)
    dterm = jnp.zeros((size,), jnp.float32)
    total = term
    dtotal = dterm
    for order in range(1, taylor_order + 1):
        nterm = jnp.dot(hess, term, precision=lax.Precision.HIGHEST) / order
        dterm = (
            jnp.dot(dhess, term, precision=lax.Precision.HIGHEST)
            + jnp.dot(hess, dterm, precision=lax.Precision.HIGHEST)
        ) / order
        term = nterm
        total = total + term
        dtotal = dtotal + dterm
    return (total, dtotal)


def local(site_tensor, site_tangent, left_env, right_env, mpo, dissipation):
    rows_here, physical, cols_here = site_tensor.shape
    channels = mpo.shape[0]
    left_whole = lax.all_gather(left_env, "col", axis=1, tiled=True)
    right_whole = lax.all_gather(right_env, "row", axis=0, tiled=True)

    def apply(stacked):
        panels = stacked.shape[1]
        whole = lax.all_gather(stacked.astype(jnp.bfloat16), "row", axis=0, tiled=True)
        flat = whole.reshape(whole.shape[0], panels * physical * cols_here)
        left_three = left_whole.reshape(rows_here, flat.shape[0], channels)
        mixed = lax.dot_general(
            left_three, flat, (((1,), (0,)), ((), ())), preferred_element_type=jnp.float32
        )
        mixed = mixed.astype(jnp.bfloat16).reshape(rows_here, channels, panels, physical, cols_here)
        channel = jnp.einsum("awspr,wvpq->asqrv", mixed, mpo, preferred_element_type=jnp.float32)
        channel = channel.astype(jnp.bfloat16).reshape(
            rows_here * panels * physical, cols_here * channels
        )
        partial_rows = lax.dot_general(
            channel, right_whole, (((1,), (1,)), ((), ())), preferred_element_type=jnp.float32
        )
        partial_rows = partial_rows.reshape(rows_here, panels, physical, partial_rows.shape[1])
        summed = lax.psum_scatter(partial_rows, "col", scatter_dimension=3, tiled=True)
        return summed - dissipation[None, None, :, None] * stacked

    primal = site_tensor.astype(jnp.float32)
    tangent = site_tangent.astype(jnp.float32)
    starting = lax.psum(jnp.stack([inner(primal, primal), inner(primal, tangent)]), ("row", "col"))
    norm_site = jnp.sqrt(starting[0])
    norm_tangent = starting[1] / norm_site
    basis = [primal / norm_site]
    tangents = [(tangent - basis[0] * norm_tangent) / norm_site]
    hess = jnp.zeros((KRYLOV, KRYLOV), jnp.float32)
    dhess = jnp.zeros((KRYLOV, KRYLOV), jnp.float32)
    for level in range(KRYLOV):
        image = apply(basis[level][:, None])[:, 0]
        dimage = apply(tangents[level][:, None])[:, 0]
        counted = level + 1
        locals_list = [inner(vector, image) for vector in basis]
        locals_list = locals_list + [inner(vector, image) for vector in tangents]
        locals_list = locals_list + [inner(vector, dimage) for vector in basis]
        totals = lax.psum(jnp.stack(locals_list), ("row", "col"))
        coeffs = totals[:counted]
        across = totals[counted : 2 * counted]
        along = totals[2 * counted : 3 * counted]
        dcoeffs = across + along
        hess = hess.at[:counted, level].set(coeffs)
        dhess = dhess.at[:counted, level].set(dcoeffs)
        if level + 1 < KRYLOV:
            residual = image
            dresidual = dimage
            for index in range(counted):
                residual = residual - coeffs[index] * basis[index]
                dresidual = (
                    dresidual - dcoeffs[index] * basis[index] - coeffs[index] * tangents[index]
                )
            paired = lax.psum(
                jnp.stack([inner(residual, residual), inner(residual, dresidual)]), ("row", "col")
            )
            squared = paired[0]
            mixed_term = paired[1]
            height = jnp.sqrt(squared)
            dheight = mixed_term / height
            newvec = residual / height
            basis.append(newvec)
            tangents.append((dresidual - newvec * dheight) / height)
            hess = hess.at[level + 1, level].set(height)
            dhess = dhess.at[level + 1, level].set(dheight)
    coeff, dcoeff = taylor(hess, dhess)
    spread = jnp.zeros_like(primal)
    dspread = jnp.zeros_like(primal)
    for index in range(KRYLOV):
        spread = spread + coeff[index] * basis[index]
        dspread = dspread + coeff[index] * tangents[index] + dcoeff[index] * basis[index]
    evolved = norm_site * spread
    evolved_tangent = norm_tangent * spread + norm_site * dspread
    return (evolved, evolved_tangent)


def solution(mesh):
    in_specs = (
        P("row", None, "col"),
        P("row", None, "col"),
        P("row", "col"),
        P("row", "col"),
        P(),
        P(),
    )
    out_specs = (P("row", None, "col"), P("row", None, "col"))
    return jax.shard_map(local, mesh=mesh, in_specs=in_specs, out_specs=out_specs, check_vma=False)
```

profile of v0, /device:TPU:1, one launch (start us, length us, event | category | flops | bytes accessed | tf_op | source)
XLA Modules:
  0.0 1113.4 jit_solution(7619003044250572234)
XLA Ops:
  8.7 1.6 fusion.97
  11.6 81.9 %psum.42 = f32[2]{0:T(128)S(1)} all-reduce(f32[2]{0:T(128)S(1)} %pad_maximum_fusion), channel_id=1, replica_groups=mesh['row'=16,'col'=16] {'row','col'}, use_global_device_ids=true, to_apply=%region_2.0 | all-reduce | flops 2 | bytes 16 | tf_op jit(solution)/shard_map/psum | solution.py:60
  96.4 18.8 %all-gather = bf16[1024,4,64]{2,1,0:T(4,128)(2,1)S(1)} all-gather(bf16[64,4,64]{2,1,0:T(4,128)(2,1)S(1)} %get-tuple-element.182), channel_id=2, replica_groups=mesh['row'=16,'col'=16] {'row'}, dimensions={0}, use_global_device_ids=true | all-gather | bytes 557056 | tf_op jit(solution)/shard_map/all_gather | solution.py:40
  116.0 4.8 copy.120
  120.8 4.5 copy.122
  125.3 1.5 fusion.36
  126.9 2.0 reshape.439
  129.8 1.7 copy.125
  131.6 2.9 fusion.13
  135.4 2.1 reshape.601
  137.6 18.6 %all-gather.1 = bf16[1024,4,64]{2,1,0:T(4,128)(2,1)S(1)} all-gather(bf16[64,4,64]{2,1,0:T(4,128)(2,1)S(1)} %get-tuple-element.181), channel_id=3, replica_groups=mesh['row'=16,'col'=16] {'row'}, dimensions={0}, use_global_device_ids=true | all-gather | bytes 557056 | tf_op jit(solution)/shard_map/all_gather | solution.py:40
  157.6 1.8 fusion.37
  159.9 1.9 fusion.31
  161.8 3.6 copy.133
  165.4 2.5 fusion.16
  168.0 1.8 copy.212
  169.7 3.3 reshape.603
  173.1 37.3 %reduce-scatter.19.cloned.1.call-done = f32[64,256]{1,0:T(8,128)} async-done(((f32[1024,256]{1,0:T(8,128)}), f32[64,256]{1,0:T(8,128)}) %reduce-scatter.19.cloned.1.call-update) | async-done | bytes 65552
  211.4 80.8 %reduce-scatter.21.cloned.1.call-done = f32[64,256]{1,0:T(8,128)} async-done(((f32[1024,256]{1,0:T(8,128)}), f32[64,256]{1,0:T(8,128)}) %reduce-scatter.21.cloned.1.call-update) | async-done | bytes 65552
  294.2 2.0 pad_maximum_fusion.1
  296.1 77.2 %psum.43 = f32[3]{0:T(128)S(1)} all-reduce(f32[3]{0:T(128)S(1)} %pad_maximum_fusion.1), channel_id=1, replica_groups=mesh['row'=16,'col'=16] {'row','col'}, use_global_device_ids=true, to_apply=%region_8.0 | all-reduce | flops 3 | bytes 24 | tf_op jit(solution)/shard_map/psum | solution.py:74
  378.1 73.2 %psum.44 = f32[2]{0:T(128)S(1)} all-reduce(f32[2]{0:T(128)S(1)} %pad_maximum_fusion.2), channel_id=1, replica_groups=mesh['row'=16,'col'=16] {'row','col'}, use_global_device_ids=true, to_apply=%region_11.0 | all-reduce | flops 2 | bytes 16 | tf_op jit(solution)/shard_map/psum | solution.py:89
  453.9 18.9 %all-gather.2 = bf16[1024,4,64]{2,1,0:T(4,128)(2,1)S(1)} all-gather(bf16[64,4,64]{2,1,0:T(4,128)(2,1)S(1)} %get-tuple-element.180), channel_id=4, replica_groups=mesh['row'=16,'col'=16] {'row'}, dimensions={0}, use_global_device_ids=true | all-gather | bytes 557056 | tf_op jit(solution)/shard_map/all_gather | solution.py:40
  474.1 3.3 fusion.38
  477.5 2.0 reshape.447
  479.5 2.8 fusion.32
  482.2 3.6 copy.141
  485.9 2.5 fusion.19
  488.4 1.8 copy.214
  490.2 3.2 reshape.605
  493.5 18.4 %all-gather.3 = bf16[1024,4,64]{2,1,0:T(4,128)(2,1)S(1)} all-gather(bf16[64,4,64]{2,1,0:T(4,128)(2,1)} %get-tuple-element.173), channel_id=5, replica_groups=mesh['row'=16,'col'=16] {'row'}, dimensions={0}, use_global_device_ids=true | all-gather | bytes 557056 | tf_op jit(solution)/shard_map/all_gather | solution.py:40
  513.3 3.3 fusion.39
  516.6 2.0 reshape.450
  518.6 2.8 fusion.33
  521.4 3.6 copy.149
  525.0 2.5 fusion.22
  527.6 1.8 copy.216
  529.3 3.2 reshape.607
  532.6 33.9 %reduce-scatter.23.cloned.1.call-done = f32[64,256]{1,0:T(8,128)} async-done(((f32[1024,256]{1,0:T(8,128)}), f32[64,256]{1,0:T(8,128)}) %reduce-scatter.23.cloned.1.call-update) | async-done | bytes 65552
  567.6 80.8 %reduce-scatter.25.cloned.1.call-done = f32[64,256]{1,0:T(8,128)} async-done(((f32[1024,256]{1,0:T(8,128)}), f32[64,256]{1,0:T(8,128)}) %reduce-scatter.25.cloned.1.call-update) | async-done | bytes 65552
  650.4 3.9 stack.106
  654.3 77.2 %psum.45 = f32[6]{0:T(128)S(1)} all-reduce(f32[6]{0:T(128)S(1)} %stack.106), channel_id=1, replica_groups=mesh['row'=16,'col'=16] {'row','col'}, use_global_device_ids=true, to_apply=%region_20.0 | all-reduce | flops 6 | bytes 48 | tf_op jit(solution)/shard_map/psum | solution.py:74
  732.8 3.4 multiply_reduce_fusion.1
  737.5 73.3 %psum.46 = f32[2]{0:T(128)S(1)} all-reduce(f32[2]{0:T(128)S(1)} %pad_maximum_fusion.3), channel_id=1, replica_groups=mesh['row'=16,'col'=16] {'row','col'}, use_global_device_ids=true, to_apply=%region_23.0 | all-reduce | flops 2 | bytes 16 | tf_op jit(solution)/shard_map/psum | solution.py:89
  813.4 18.9 %all-gather.5 = bf16[1024,4,64]{2,1,0:T(4,128)(2,1)S(1)} all-gather(bf16[64,4,64]{2,1,0:T(4,128)(2,1)S(1)} %get-tuple-element.168), channel_id=7, replica_groups=mesh['row'=16,'col'=16] {'row'}, dimensions={0}, use_global_device_ids=true | all-gather | bytes 557056 | tf_op jit(solution)/shard_map/all_gather | solution.py:40
  833.7 3.3 fusion.41
  837.0 2.0 reshape.460
  839.1 2.8 fusion.35
  841.8 3.6 copy.165
  845.4 2.5 fusion.28
  848.0 1.8 copy.220
  849.7 3.2 reshape.611
  853.1 18.5 %all-gather.4 = bf16[1024,4,64]{2,1,0:T(4,128)(2,1)S(1)} all-gather(bf16[64,4,64]{2,1,0:T(4,128)(2,1)} %get-tuple-element.179), channel_id=6, replica_groups=mesh['row'=16,'col'=16] {'row'}, dimensions={0}, use_global_device_ids=true | all-gather | bytes 557056 | tf_op jit(solution)/shard_map/all_gather | solution.py:40
  872.9 3.3 fusion.40
  876.3 2.0 reshape.457
  878.3 2.8 fusion.34
  881.1 3.6 copy.157
  884.7 2.5 fusion.25
  888.2 2.1 reshape.609
  894.8 31.1 %reduce-scatter.29.cloned.1.call-done = f32[64,256]{1,0:T(8,128)} async-done(((f32[1024,256]{1,0:T(8,128)}), f32[64,256]{1,0:T(8,128)}) %reduce-scatter.29.cloned.1.call-update) | async-done | bytes 65552
  927.0 80.9 %reduce-scatter.27.cloned.1.call-done = f32[64,256]{1,0:T(8,128)} async-done(((f32[1024,256]{1,0:T(8,128)}), f32[64,256]{1,0:T(8,128)}) %reduce-scatter.27.cloned.1.call-update) | async-done | bytes 65552
  1010.3 5.8 stack.119
  1016.2 77.2 %psum.47 = f32[9]{0:T(128)S(1)} all-reduce(f32[9]{0:T(128)S(1)} %stack.119), channel_id=1, replica_groups=mesh['row'=16,'col'=16] {'row','col'}, use_global_device_ids=true, to_apply=%region_35.0 | all-reduce | flops 9 | bytes 72 | tf_op jit(solution)/shard_map/psum | solution.py:74
  1101.5 4.5 multiply_add_fusion
  (147 shorter events, 46.1 us)
Async XLA Ops:
  7.2 108.7 %copy-start.8 = (bf16[16,16,4,4]{1,3,2,0:T(4,128)(2,1)S(1)}, bf16[16,16,4,4]{1,3,2,0:T(4,128)(2,1)}, u32[]{:S(2)}) copy-start(bf16[16,16,4,4]{1,3,2,0:T(4,128)(2,1)} %param.32) | copy-start | bytes 24580
  7.2 108.9 %all-gather.9.cloned.1.call-start = ((), (), s32[]{:S(2)}) async-start(), calls=%async_computation.6 | async-start | bytes 2228224 | tf_op jit(solution)/shard_map/all_gather | solution.py:35
  7.9 123.7 %all-gather.11.cloned.1.call-start = ((), (), s32[]{:S(2)}) async-start(), calls=%async_computation.7 | async-start | bytes 2228224 | tf_op jit(solution)/shard_map/all_gather | solution.py:36
  8.7 201.7 %reduce-scatter.19.cloned.1.call-start = ((), (), s32[]{:S(2)}) async-start(), calls=%async_computation.8 | async-start | bytes 1114112
  116.0 43.8 %copy-start.9 = (bf16[16,16,4,4]{0,1,2,3:T(8,128)(2,1)}, bf16[16,16,4,4]{0,1,2,3:T(8,128)(2,1)S(1)}, u32[]{:S(2)}) copy-start(bf16[16,16,4,4]{0,1,2,3:T(8,128)(2,1)S(1)} %copy.124) | copy-start | bytes 24580
  125.3 3.6 copy-start.5
  137.6 20.1 %copy-start.6 = (bf16[64,1024,16]{1,0,2:T(8,128)(2,1)S(1)}, bf16[64,1024,16]{1,0,2:T(8,128)(2,1)}, u32[]{:S(2)}) copy-start(bf16[64,1024,16]{1,0,2:T(8,128)(2,1)} %copy-done.5) | copy-start | bytes 6291460
  137.6 154.6 %reduce-scatter.21.cloned.1.call-start = ((), (), s32[]{:S(2)}) async-start(), calls=%async_computation.9 | async-start | bytes 1114112
  159.9 5.6 copy-start
  169.7 123.6 %copy-start.1 = (bf16[64,4,64]{2,1,0:T(4,128)(2,1)S(1)}, bf16[64,4,64]{2,1,0:T(4,128)(2,1)}, u32[]{:S(2)}) copy-start(bf16[64,4,64]{2,1,0:T(4,128)(2,1)} %param.28) | copy-start | bytes 98308
  169.7 123.6 %copy-start.2 = (bf16[64,4,64]{2,1,0:T(4,128)(2,1)S(1)}, bf16[64,4,64]{2,1,0:T(4,128)(2,1)}, u32[]{:S(2)}) copy-start(bf16[64,4,64]{2,1,0:T(4,128)(2,1)} %param.29) | copy-start | bytes 98308
  169.7 123.6 %copy-start.10 = (f32[4]{0:T(128)S(1)}, f32[4]{0:T(128)}, u32[]{:S(2)}) copy-start(f32[4]{0:T(128)} %param.33) | copy-start | bytes 52
  173.0 393.5 %reduce-scatter.23.cloned.1.call-start = ((), (), s32[]{:S(2)}) async-start(), calls=%async_computation.10 | async-start | bytes 1114112
  493.4 154.9 %reduce-scatter.25.cloned.1.call-start = ((), (), s32[]{:S(2)}) async-start(), calls=%async_computation.11 | async-start | bytes 1114112
  532.6 393.4 %reduce-scatter.29.cloned.1.call-start = ((), (), s32[]{:S(2)}) async-start(), calls=%async_computation.13 | async-start | bytes 1114112
  736.2 77.2 %copy-start.3 = (f32[64,4,64]{2,1,0:T(4,128)}, f32[64,4,64]{2,1,0:T(4,128)S(1)}, u32[]{:S(2)}) copy-start(f32[64,4,64]{2,1,0:T(4,128)S(1)} %get-tuple-element.171) | copy-start | bytes 196612
  853.0 155.0 %reduce-scatter.27.cloned.1.call-start = ((), (), s32[]{:S(2)}) async-start(), calls=%async_computation.12 | async-start | bytes 1114112
  888.2 120.9 %copy-start.4 = (f32[64,4,64]{2,1,0:T(4,128)S(1)}, f32[64,4,64]{2,1,0:T(4,128)}, u32[]{:S(2)}) copy-start(f32[64,4,64]{2,1,0:T(4,128)} %copy-done.3) | copy-start | bytes 196612
  888.2 120.9 %copy-start.7 = (f32[64,4,64]{2,1,0:T(4,128)S(1)}, f32[64,4,64]{2,1,0:T(4,128)}, u32[]{:S(2)}) copy-start(f32[64,4,64]{2,1,0:T(4,128)} %get-tuple-element.169) | copy-start | bytes 196612
  890.3 203.3 %copy-start.11 = (f32[3,1]{0,1:T(1,128)S(1)}, f32[3,1]{0,1:T(1,128)}, u32[]{:S(2)}) copy-start(f32[3,1]{0,1:T(1,128)} %constant.327) | copy-start | bytes 40
Sparse Core Ops, SparseCore 0:
  10.5 52.1 all-gather.8
  64.5 40.9 all-gather.10
  137.7 72.6 reduce-scatter.18
  213.7 78.4 reduce-scatter.20
  493.6 72.8 reduce-scatter.22
  569.8 78.4 reduce-scatter.24
  853.1 72.8 reduce-scatter.28
  929.5 78.4 reduce-scatter.26
where the time goes:
time: 1120 us; the launch traced here: 1110 us
  blocking collectives  572 us (51%)
  waiting for transfers between devices  346 us (31%)
  local copies, waits for them, and re-layouts  98.9 us (9%)
  matrix products  52.6 us (5%)
  other arithmetic  22.7 us (2%)
  between operations  20.4 us (2%)
    unnamed x14, waiting for transfers between devices  346 us
    psum x3, blocking collectives, local(): totals = lax.psum(jnp.stack(locals_list), ('row', 'col'))  232 us
    psum x2, blocking collectives, local(): lax.psum(jnp.stack([inner(residual, residual), inner(residual, dresidual)...  146 us
    all_gather x6, blocking collectives, apply(): lax.all_gather(stacked.astype(jnp.bfloat16), 'row', axis=0, tiled=True)  112 us
    psum x1, blocking collectives, local(): lax.psum(jnp.stack([inner(primal, primal), inner(primal, tangent)]), ('ro...  81.9 us
    unnamed x43, local copies, waits for them, and re-layouts  31.9 us
  transfers between devices with their start and end apart: 8, of which 6 were waited for; matrix products, arithmetic and copies ran while one was open for 8% of the time, Pallas kernels for 0%

commit v1 on v0

--- a/solution.py
+++ b/solution.py
@@ -1,3 +1,4 @@
+import functools
 import jax
 import jax.numpy as jnp
 from jax import lax
@@ -5,6 +6,20 @@
 
 KRYLOV = 3
 taylor_order = 16
+
+
+def group_map(xx, lane_axis):
+    items = []
+    for _ in range(lax.axis_size(lane_axis)):
+        items.append(xx)
+    block_last = jnp.concatenate(
+        lax.all_to_all(jnp.stack(items, axis=0), axis_name=lane_axis, split_axis=0, concat_axis=0),
+        0,
+    )
+    return block_last
+
+
+_cut_matrix = functools.partial(group_map, lane_axis="row")
 
 
 def inner(first, second):
@@ -37,7 +52,7 @@
 
     def apply(stacked):
         panels = stacked.shape[1]
-        whole = lax.all_gather(stacked.astype(jnp.bfloat16), "row", axis=0, tiled=True)
+        whole = _cut_matrix(stacked.astype(jnp.bfloat16))
         flat = whole.reshape(whole.shape[0], panels * physical * cols_here)
         left_three = left_whole.reshape(rows_here, flat.shape[0], channels)
         mixed = lax.dot_general(

time: 1120 us -> 1140 us (1.018)
  local copies, waits for them, and re-layouts: 98.9 us -> 127 us
    all_gather x6 -> x0, blocking collectives: 112 us -> none  [apply(): lax.all_gather(stacked.astype(jnp.bfloat16), 'row', axis=0, tiled=True)]
    all_to_all x0 -> x5, blocking collectives: none -> 108 us  [group_map(): lax.all_to_all(jnp.stack(items, axis=0), axis_name=lane_axis, split_axis=...]
    unnamed x43 -> x73, local copies, waits for them, and re-layouts: 31.9 us -> 59.9 us
    unnamed x14, waiting for transfers between devices: 346 us -> 319 us
    all_to_all x0 -> x1, waiting for transfers between devices: none -> 17 us  [group_map(): lax.all_to_all(jnp.stack(items, axis=0), axis_name=lane_axis, split_axis=...]
  transfers between devices with their start and end apart: 8 -> 9, of which waited for: 6 -> 7; matrix products, arithmetic and copies ran while one was open for 8% -> 9% of each run, Pallas kernels for 0% -> 0%
where the time goes in v1:
time: 1140 us; the launch traced here: 1130 us
  blocking collectives  568 us (50%)
  waiting for transfers between devices  336 us (29%)
  local copies, waits for them, and re-layouts  127 us (11%)
  matrix products  52.4 us (5%)
  other arithmetic  21.1 us (2%)
  between operations  20.5 us (2%)
    unnamed x14, waiting for transfers between devices  319 us
    psum x3, blocking collectives, local(): totals = lax.psum(jnp.stack(locals_list), ('row', 'col'))  232 us
    psum x2, blocking collectives, local(): lax.psum(jnp.stack([inner(residual, residual), inner(residual, dresidual)...  147 us
    all_to_all x5, blocking collectives, group_map(): lax.all_to_all(jnp.stack(items, axis=0), axis_name=lane_axis, split_axis=...  108 us
    psum x1, blocking collectives, local(): lax.psum(jnp.stack([inner(primal, primal), inner(primal, tangent)]), ('ro...  81.9 us
    unnamed x73, local copies, waits for them, and re-layouts  59.9 us
  transfers between devices with their start and end apart: 9, of which 7 were waited for; matrix products, arithmetic and copies ran while one was open for 9% of the time, Pallas kernels for 0%

profile of v1, /device:TPU:1, one launch (start us, length us, event | category | flops | bytes accessed | tf_op | source)
XLA Modules:
  0.0 1130.2 jit_solution(890827312399497373)
XLA Ops:
  11.6 81.9 %psum.42 = f32[2]{0:T(128)S(1)} all-reduce(f32[2]{0:T(128)S(1)} %pad_maximum_fusion), channel_id=1, replica_groups=mesh['row'=16,'col'=16] {'row','col'}, use_global_device_ids=true, to_apply=%region_2.0 | all-reduce | flops 2 | bytes 16 | tf_op jit(solution)/shard_map/psum | solution.py:75
  98.3 4.7 all-to-all-start
  103.2 17.0 %all-to-all-done = bf16[16,2,8192]{2,1,0:T(2,128)(2,1)S(1)} async-done(((bf16[16,2,8192]{2,1,0:T(2,128)(2,1)}), bf16[16,2,8192]{2,1,0:T(2,128)(2,1)S(1)}, u32[]{:S(2)}, u32[]{:S(2)}) %all-to-all-start) | async-done | bytes 524320 | tf_op jit(solution)/shard_map/all_to_all | solution.py:16
  121.6 4.8 copy.74
  126.3 4.5 copy.75
  132.3 2.0 reshape.438
  137.1 2.9 fusion.13
  140.9 2.1 reshape.589
  145.1 20.5 %all_to_all.30 = bf16[16,2,8192]{2,1,0:T(2,128)(2,1)} all-to-all(bf16[16,2,8192]{2,1,0:T(2,128)(2,1)} %reshape.603), channel_id=1, replica_groups=mesh['row'=16,'col'=16] {'row'}, dimensions={0} | all-to-all | bytes 1048576 | tf_op jit(solution)/shard_map/all_to_all | solution.py:16
  165.6 2.7 reshape.604
  172.0 1.9 fusion.31
  173.9 3.6 copy.84
  177.5 2.5 fusion.16
  180.1 1.8 copy.144
  181.8 3.3 reshape.591
  185.2 28.4 %reduce-scatter.19.cloned.1.call-done = f32[64,256]{1,0:T(8,128)} async-done(((f32[1024,256]{1,0:T(8,128)}), f32[64,256]{1,0:T(8,128)}) %reduce-scatter.19.cloned.1.call-update) | async-done | bytes 65552
  214.6 80.7 %reduce-scatter.21.cloned.1.call-done = f32[64,256]{1,0:T(8,128)} async-done(((f32[1024,256]{1,0:T(8,128)}), f32[64,256]{1,0:T(8,128)}) %reduce-scatter.21.cloned.1.call-update) | async-done | bytes 65552
  297.1 2.0 pad_maximum_fusion.1
  299.1 77.2 %psum.43 = f32[3]{0:T(128)S(1)} all-reduce(f32[3]{0:T(128)S(1)} %pad_maximum_fusion.1), channel_id=1, replica_groups=mesh['row'=16,'col'=16] {'row','col'}, use_global_device_ids=true, to_apply=%region_8.0 | all-reduce | flops 3 | bytes 24 | tf_op jit(solution)/shard_map/psum | solution.py:89
  380.9 73.3 %psum.44 = f32[2]{0:T(128)S(1)} all-reduce(f32[2]{0:T(128)S(1)} %pad_maximum_fusion.2), channel_id=1, replica_groups=mesh['row'=16,'col'=16] {'row','col'}, use_global_device_ids=true, to_apply=%region_11.0 | all-reduce | flops 2 | bytes 16 | tf_op jit(solution)/shard_map/psum | solution.py:104
  458.8 23.2 %all_to_all.31 = bf16[16,2,8192]{2,1,0:T(2,128)(2,1)} all-to-all(bf16[16,2,8192]{2,1,0:T(2,128)(2,1)} %reshape.607), channel_id=1, replica_groups=mesh['row'=16,'col'=16] {'row'}, dimensions={0} | all-to-all | bytes 1048576 | tf_op jit(solution)/shard_map/all_to_all | solution.py:16
  482.0 2.7 reshape.608
  486.2 3.3 fusion.38
  489.5 2.0 reshape.444
  491.5 2.8 fusion.32
  494.3 3.6 copy.90
  497.9 2.5 fusion.19
  500.5 1.8 copy.146
  502.2 3.3 reshape.593
  507.6 20.5 %all_to_all.32 = bf16[16,2,8192]{2,1,0:T(2,128)(2,1)} all-to-all(bf16[16,2,8192]{2,1,0:T(2,128)(2,1)} %reshape.605), channel_id=1, replica_groups=mesh['row'=16,'col'=16] {'row'}, dimensions={0} | all-to-all | bytes 1048576 | tf_op jit(solution)/shard_map/all_to_all | solution.py:16
  528.1 2.7 reshape.606
  532.3 3.3 fusion.39
  535.6 2.0 reshape.446
  537.6 2.8 fusion.33
  540.4 3.6 copy.96
  544.0 2.5 fusion.22
  548.3 3.2 reshape.595
  551.6 24.8 %reduce-scatter.23.cloned.1.call-done = f32[64,256]{1,0:T(8,128)} async-done(((f32[1024,256]{1,0:T(8,128)}), f32[64,256]{1,0:T(8,128)}) %reduce-scatter.23.cloned.1.call-update) | async-done | bytes 65552
  577.4 80.8 %reduce-scatter.25.cloned.1.call-done = f32[64,256]{1,0:T(8,128)} async-done(((f32[1024,256]{1,0:T(8,128)}), f32[64,256]{1,0:T(8,128)}) %reduce-scatter.25.cloned.1.call-update) | async-done | bytes 65552
  660.1 3.9 stack.92
  664.0 77.2 %psum.45 = f32[6]{0:T(128)S(1)} all-reduce(f32[6]{0:T(128)S(1)} %stack.92), channel_id=1, replica_groups=mesh['row'=16,'col'=16] {'row','col'}, use_global_device_ids=true, to_apply=%region_20.0 | all-reduce | flops 6 | bytes 48 | tf_op jit(solution)/shard_map/psum | solution.py:89
  742.5 3.3 multiply_reduce_fusion.1
  747.1 73.3 %psum.46 = f32[2]{0:T(128)S(1)} all-reduce(f32[2]{0:T(128)S(1)} %pad_maximum_fusion.3), channel_id=1, replica_groups=mesh['row'=16,'col'=16] {'row','col'}, use_global_device_ids=true, to_apply=%region_23.0 | all-reduce | flops 2 | bytes 16 | tf_op jit(solution)/shard_map/psum | solution.py:104
  825.0 23.0 %all_to_all.33 = bf16[16,2,8192]{2,1,0:T(2,128)(2,1)} all-to-all(bf16[16,2,8192]{2,1,0:T(2,128)(2,1)} %reshape.609), channel_id=1, replica_groups=mesh['row'=16,'col'=16] {'row'}, dimensions={0} | all-to-all | bytes 1048576 | tf_op jit(solution)/shard_map/all_to_all | solution.py:16
  848.0 2.7 reshape.610
  852.3 3.3 fusion.41
  855.5 2.0 reshape.454
  857.6 2.8 fusion.35
  860.3 3.6 copy.108
  864.0 2.5 fusion.28
  868.3 3.3 reshape.599
  873.6 20.6 %all_to_all.34 = bf16[16,2,8192]{2,1,0:T(2,128)(2,1)} all-to-all(bf16[16,2,8192]{2,1,0:T(2,128)(2,1)} %reshape.611), channel_id=1, replica_groups=mesh['row'=16,'col'=16] {'row'}, dimensions={0} | all-to-all | bytes 1048576 | tf_op jit(solution)/shard_map/all_to_all | solution.py:16
  894.2 2.7 reshape.612
  898.4 3.3 fusion.40
  901.7 2.0 reshape.452
  903.8 2.8 fusion.34
  906.5 3.6 copy.102
  910.1 2.5 fusion.25
  913.6 2.1 reshape.597
  920.3 22.2 %reduce-scatter.29.cloned.1.call-done = f32[64,256]{1,0:T(8,128)} async-done(((f32[1024,256]{1,0:T(8,128)}), f32[64,256]{1,0:T(8,128)}) %reduce-scatter.29.cloned.1.call-update) | async-done | bytes 65552
  943.5 80.9 %reduce-scatter.27.cloned.1.call-done = f32[64,256]{1,0:T(8,128)} async-done(((f32[1024,256]{1,0:T(8,128)}), f32[64,256]{1,0:T(8,128)}) %reduce-scatter.27.cloned.1.call-update) | async-done | bytes 65552
  1026.5 5.8 stack.107
  1032.3 77.2 %psum.47 = f32[9]{0:T(128)S(1)} all-reduce(f32[9]{0:T(128)S(1)} %stack.107), channel_id=1, replica_groups=mesh['row'=16,'col'=16] {'row','col'}, use_global_device_ids=true, to_apply=%region_35.0 | all-reduce | flops 9 | bytes 72 | tf_op jit(solution)/shard_map/psum | solution.py:89
  1117.5 3.9 multiply_add_fusion
  (178 shorter events, 69.9 us)
Async XLA Ops:
  7.2 114.4 %all-gather.3.cloned.1.call-start = ((), (), s32[]{:S(2)}) async-start(), calls=%async_computation.12 | async-start | bytes 2228224 | tf_op jit(solution)/shard_map/all_gather | solution.py:50
  7.9 129.2 %all-gather.5.cloned.1.call-start = ((), (), s32[]{:S(2)}) async-start(), calls=%async_computation.13 | async-start | bytes 2228224 | tf_op jit(solution)/shard_map/all_gather | solution.py:51
  10.2 92.9 %copy-start.10 = (bf16[16,16,4,4]{1,3,2,0:T(4,128)(2,1)S(1)}, bf16[16,16,4,4]{1,3,2,0:T(4,128)(2,1)}, u32[]{:S(2)}) copy-start(bf16[16,16,4,4]{1,3,2,0:T(4,128)(2,1)} %param.32) | copy-start | bytes 24580
  98.3 21.9 %all-to-all-start = ((bf16[16,2,8192]{2,1,0:T(2,128)(2,1)}), bf16[16,2,8192]{2,1,0:T(2,128)(2,1)S(1)}, u32[]{:S(2)}, u32[]{:S(2)}) async-start(bf16[16,2,8192]{2,1,0:T(2,128)(2,1)} %reshape.601), calls=%async_computation | async-start | bytes 1048576 | tf_op jit(solution)/shard_map/all_to_all | solution.py:16
  103.0 110.5 %reduce-scatter.19.cloned.1.call-start = ((), (), s32[]{:S(2)}) async-start(), calls=%async_computation.14 | async-start | bytes 1114112
  103.2 68.8 %copy-start.11 = (bf16[16,16,4,4]{0,1,2,3:T(8,128)(2,1)}, bf16[16,16,4,4]{0,1,2,3:T(8,128)(2,1)S(1)}, u32[]{:S(2)}) copy-start(bf16[16,16,4,4]{0,1,2,3:T(8,128)(2,1)S(1)} %copy.77) | copy-start | bytes 24580
  130.8 1.5 copy-start.5
  143.1 152.2 %reduce-scatter.21.cloned.1.call-start = ((), (), s32[]{:S(2)}) async-start(), calls=%async_computation.15 | async-start | bytes 1114112
  145.1 24.7 %copy-start.6 = (bf16[64,1024,16]{1,0,2:T(8,128)(2,1)S(1)}, bf16[64,1024,16]{1,0,2:T(8,128)(2,1)}, u32[]{:S(2)}) copy-start(bf16[64,1024,16]{1,0,2:T(8,128)(2,1)} %copy-done.5) | copy-start | bytes 6291460
  172.0 5.6 copy-start
  181.8 114.5 %copy-start.1 = (bf16[64,4,64]{2,1,0:T(4,128)(2,1)S(1)}, bf16[64,4,64]{2,1,0:T(4,128)(2,1)}, u32[]{:S(2)}) copy-start(bf16[64,4,64]{2,1,0:T(4,128)(2,1)} %param.28) | copy-start | bytes 98308
  181.8 114.6 %copy-start.2 = (bf16[64,4,64]{2,1,0:T(4,128)(2,1)S(1)}, bf16[64,4,64]{2,1,0:T(4,128)(2,1)}, u32[]{:S(2)}) copy-start(bf16[64,4,64]{2,1,0:T(4,128)(2,1)} %param.29) | copy-start | bytes 98308
  181.8 114.6 %copy-start.12 = (f32[4]{0:T(128)S(1)}, f32[4]{0:T(128)}, u32[]{:S(2)}) copy-start(f32[4]{0:T(128)} %param.33) | copy-start | bytes 52
  185.1 391.2 %reduce-scatter.23.cloned.1.call-start = ((), (), s32[]{:S(2)}) async-start(), calls=%async_computation.16 | async-start | bytes 1114112
  502.2 3.3 copy-start.8
  505.5 152.7 %reduce-scatter.25.cloned.1.call-start = ((), (), s32[]{:S(2)}) async-start(), calls=%async_computation.17 | async-start | bytes 1114112
  551.6 390.9 %reduce-scatter.29.cloned.1.call-start = ((), (), s32[]{:S(2)}) async-start(), calls=%async_computation.19 | async-start | bytes 1114112
  745.8 77.2 %copy-start.3 = (f32[64,4,64]{2,0,1:T(8,128)}, f32[64,4,64]{2,0,1:T(8,128)S(1)}, u32[]{:S(2)}) copy-start(f32[64,4,64]{2,0,1:T(8,128)S(1)} %get-tuple-element.171) | copy-start | bytes 196612
  868.3 3.3 copy-start.9
  871.5 152.9 %reduce-scatter.27.cloned.1.call-start = ((), (), s32[]{:S(2)}) async-start(), calls=%async_computation.18 | async-start | bytes 1114112
  913.6 111.9 %copy-start.4 = (f32[64,4,64]{2,0,1:T(8,128)S(1)}, f32[64,4,64]{2,0,1:T(8,128)}, u32[]{:S(2)}) copy-start(f32[64,4,64]{2,0,1:T(8,128)} %copy-done.3) | copy-start | bytes 196612
  913.6 111.9 %copy-start.7 = (f32[64,4,64]{2,0,1:T(8,128)S(1)}, f32[64,4,64]{2,0,1:T(8,128)}, u32[]{:S(2)}) copy-start(f32[64,4,64]{2,0,1:T(8,128)} %get-tuple-element.169) | copy-start | bytes 196612
  915.8 194.0 %copy-start.13 = (f32[3,1]{0,1:T(1,128)S(1)}, f32[3,1]{0,1:T(1,128)}, u32[]{:S(2)}) copy-start(f32[3,1]{0,1:T(1,128)} %constant.327) | copy-start | bytes 40
Sparse Core Ops, SparseCore 0:
  10.5 52.1 all-gather.2
  64.5 40.7 all-gather.4
  143.2 70.3 reduce-scatter.18
  216.9 78.3 reduce-scatter.20
  505.6 70.6 reduce-scatter.22
  579.7 78.4 reduce-scatter.24
  871.7 70.7 reduce-scatter.28
  945.9 78.4 reduce-scatter.26
